TPU v7x, 32 devices: a whole 2x2x4 slice. The times are simulated.
32 devices in a mesh: row: 4 (over y, x), col: 8 (over z, core).
Axes of the slice: x: 2, y: 2, z: 4, core: 2. Of those that a mesh axis runs over, the one named last changes fastest.
Arguments:
- left_blocks: bfloat16 [96, 32, 128, 128], P('col', 'row'), may hold values from -0.5 to 0.5
- left_cols: int32 [96, 32], P('col', 'row'), may hold values from 0 to 511, as said below
- right_blocks: bfloat16 [512, 4, 128, 128], P('col', 'row'), may hold values from -6 to 6
- right_cols: int32 [512, 4], P('col', 'row'), may hold values from 0 to 127, as said below
- keep_cols: int32 [96, 16], P('col', 'row'), may hold values from 0 to 127, as said below
Outputs:
- product_blocks: bfloat16 [96, 16, 128, 128], P('col', 'row')
Inputs may be any that keep to these rules, and one draw needn't show every extreme that they name: `left_cols`: slot s of every block row names a block column in [(s // 4) * 64, (s // 4 + 1) * 64); the 4 slots of one range name distinct block columns. `right_cols`: entry [K, n] names a block column in [n * 32, (n + 1) * 32). `keep_cols`: slot k of every block row names a block column in [(k // 4) * 32, (k // 4 + 1) * 32); the 4 slots of one range name distinct block columns.
All inputs are finite; a program needn't handle non-finite values.
Results may differ from a plain program's by a relative error of at most 0.001.
Values may be sent and summed in bfloat16 or wider, within the bound.
No kernel may reach another device: no remote copies, remote signals or barrier semaphores. Data moves between devices by JAX's collectives and lax.ppermute only.
A program may use at most 192 MiB of HBM per device.

v0:
```python
import jax
import jax.numpy as jnp
from jax import lax
from jax.sharding import PartitionSpec as P

NJR = 32


def slot_index(targets, kept):
    match = targets[:, :, None] == kept[:, None, :]
    found = jnp.any(match, axis=2)
    position = jnp.sum(
        match.astype(jnp.int32) * jnp.arange(kept.shape[1], dtype=jnp.int32)[None, None, :], axis=2
    )
    return jnp.where(found, position, kept.shape[1])


def place_terms(summed, terms, targets, kept):
    index = slot_index(targets, kept)
    rows = jnp.broadcast_to(jnp.arange(terms.shape[0], dtype=jnp.int32)[:, None], index.shape)
    return summed.at[rows, index].add(terms, mode="drop")


def local(left_blocks, left_cols, right_blocks, right_cols, keep_cols):
    row_rank = lax.axis_index("row")
    kept = keep_cols - row_rank * NJR
    panel_blocks, panel_cols = (
        lax.all_gather(left_blocks, "row", axis=1, tiled=True),
        lax.all_gather(left_cols, "row", axis=1, tiled=True),
    )
    start_sum = jnp.zeros(
        (panel_blocks.shape[0], keep_cols.shape[1], panel_blocks.shape[2], panel_blocks.shape[3]),
        jnp.float32,
    )
    start = jnp.int32(0)
    piece_blocks = lax.all_gather(right_blocks, "col", axis=0, tiled=True)
    piece_cols = lax.all_gather(right_cols, "col", axis=0, tiled=True)
    local_index = panel_cols - start
    chosen = jnp.take(piece_blocks[:, 0], local_index, axis=0)
    targets = jnp.take(piece_cols[:, 0], local_index, axis=0) - row_rank * NJR
    terms = jnp.einsum("isxy,isyz->isxz", panel_blocks, chosen, preferred_element_type=jnp.float32)
    summed = place_terms(start_sum, terms, targets, kept)
    return summed.astype(jnp.bfloat16)


def solution(mesh):
    in_specs = (
        P("col", "row", None, None),
        P("col", "row"),
        P("col", "row", None, None),
        P("col", "row"),
        P("col", "row"),
    )
    out_specs = P("col", "row", None, None)
    return jax.shard_map(local, mesh=mesh, in_specs=in_specs, out_specs=out_specs, check_vma=False)
```

profile of v0, /device:TPU:0, one launch (start us, length us, event | category | flops | bytes accessed | tf_op | source)
XLA Modules:
  0.0 393.2 jit_solution(15735401039370473601)
XLA Ops:
  6.5 0.0 copy-start
  6.5 0.0 all-gather.3.cloned.1.call-start
  6.5 0.7 all-gather.3.cloned.1.call-update
  7.3 0.0 all-gather.5.cloned.1.call-start
  7.3 0.7 all-gather.5.cloned.1.call-update
  8.0 9.8 %all_gather.12 = s32[12,32]{0,1:T(8,128)S(1)} all-gather(s32[12,8]{0,1:T(8,128)} %param.6), channel_id=1, replica_groups=mesh['row'=4,'col'=8] {'row'}, dimensions={1}, use_global_device_ids=true | all-gather | bytes 1920 | tf_op jit(solution)/shard_map/all_gather | solution.py:29
  17.8 0.1 copy.21
  17.9 0.1 reshape.46
  18.0 1.2 dynamic-slice
  19.9 0.8 bitcast_dynamic-update-slice_fusion
  20.7 11.1 %all-reduce = s32[512]{0:T(512)S(1)} all-reduce(s32[512]{0:T(512)S(1)} %bitcast_dynamic-update-slice_fusion), channel_id=1, replica_groups=mesh['row'=4,'col'=8] {'col'}, use_global_device_ids=true, to_apply=%add | all-reduce | flops 512 | bytes 4096 | tf_op jit(solution)/shard_map/squeeze | solution.py:40
  31.7 2.8 gather_fusion
  34.5 0.1 reshape.45
  34.6 0.0 copy-done
  34.6 0.1 copy.24
  34.7 0.1 fusion.4
  34.8 0.1 compare_reduce_fusion
  34.9 0.1 reshape.60
  35.0 127.9 %all-gather.3.cloned.1.call-done = bf16[512,1,128,128]{3,2,1,0:T(8,128)(2,1)} async-done(((bf16[64,1,128,128]{3,2,1,0:T(8,128)(2,1)}), bf16[512,1,128,128]{3,2,1,0:T(8,128)(2,1)}) %all-gather.3.cloned.1.call-update) | async-done | bytes 16777232 | tf_op jit(solution)/shard_map/all_gather | solution.py:36
  162.9 16.8 %gather_fusion.1 = bf16[384,128,128]{2,1,0:T(8,128)(2,1)} fusion(bf16[512,128,128]{2,1,0:T(8,128)(2,1)} %bitcast.17, s32[1024]{0:T(1024)S(1)} %pad_clamp_fusion), kind=kCustom, calls=%fused_computation.1 | custom fusion | bytes 25167360 | tf_op jit(solution)/shard_map/jit(_take)/gather | solution.py:39
  179.8 16.6 %copy.25 = bf16[12,32,128,128]{2,3,1,0:T(8,128)(2,1)} copy(bf16[12,32,128,128]{3,2,1,0:T(8,128)(2,1)} %bitcast.16) | data formatting | bytes 25165824 | tf_op jit(solution)/shard_map/jit(_take)/gather | solution.py:39
  196.4 89.0 %all-gather.5.cloned.1.call-done = bf16[12,32,128,128]{3,2,1,0:T(8,128)(2,1)} async-done(((bf16[12,8,128,128]{3,2,1,0:T(8,128)(2,1)}), bf16[12,32,128,128]{3,2,1,0:T(8,128)(2,1)}) %all-gather.5.cloned.1.call-update) | async-done | bytes 12582928 | tf_op jit(solution)/shard_map/all_gather | solution.py:28
  285.4 22.1 %fusion = f32[12,32,128,128]{3,2,1,0:T(8,128)} fusion(bf16[12,32,128,128]{3,2,1,0:T(8,128)(2,1)} %all-gather.5.cloned.1.call-done, bf16[12,32,128,128]{2,3,1,0:T(8,128)(2,1)} %copy.25, pred[12,32]{1,0:T(8,128)(4,1)S(1)} %get-tuple-element.6), kind=kOutput, calls=%fused_computation.3 | convolution fusion | flops 1616904192 | bytes 50332032 | tf_op jit(solution)/shard_map/isxy,isyz->isxz/dot_general | solution.py:41
  307.5 24.7 %copy.26 = f32[384,128,128]{2,1,0:T(8,128)} copy(f32[384,128,128]{1,2,0:T(8,128)} %bitcast.15) | data formatting | bytes 50331648 | tf_op jit(solution)/shard_map/isxy,isyz->isxz/dot_general | solution.py:41
  332.2 0.4 broadcast_in_dim.38
  332.5 52.4 %scatter_fusion = f32[12,4,128,128]{3,2,1,0:T(8,128)S(1)} fusion(f32[12,4,128,128]{3,2,1,0:T(8,128)S(1)} %broadcast_in_dim.38, s32[384]{0:T(512)S(1)} %reshape.60, f32[384,128,128]{2,1,0:T(8,128)} %copy.26), kind=kCustom, calls=%fused_computation.2 | custom fusion | flops 6291456 | bytes 75500544 | tf_op jit(solution)/shard_map/scatter-add | solution.py:21
  384.9 1.4 convert_element_type.4
  (6 shorter events, 0.0 us)
Async XLA Ops:
  6.5 28.1 %copy-start = (s32[12,4]{0,1:T(4,128)S(1)}, s32[12,4]{0,1:T(4,128)}, u32[]{:S(2)}) copy-start(s32[12,4]{0,1:T(4,128)} %param.9) | copy-start | bytes 580
  6.5 156.4 %all-gather.3.cloned.1.call-start = ((), (), s32[]{:S(2)}) async-start(), calls=%async_computation | async-start | bytes 18874368 | tf_op jit(solution)/shard_map/all_gather | solution.py:36
  7.3 278.1 %all-gather.5.cloned.1.call-start = ((), (), s32[]{:S(2)}) async-start(), calls=%async_computation.1 | async-start | bytes 15728640 | tf_op jit(solution)/shard_map/all_gather | solution.py:28
Sparse Core Ops, SparseCore 0:
  8.9 153.9 all-gather.2
  164.8 120.5 all-gather.4
where the time goes:
time: 395 us; the launch traced here: 393 us
  waiting for transfers between devices  218 us (55%)
  local copies, waits for them, and re-layouts  63.7 us (16%)
  other arithmetic  54 us (14%)
  matrix products  22.1 us (6%)
  blocking collectives  20.9 us (5%)
  between operations  14.1 us (4%)
    all_gather x1, waiting for transfers between devices, local(): piece_blocks = lax.all_gather(right_blocks, 'col', axis=0, tiled=True)  128 us
    all_gather x1, waiting for transfers between devices, local(): lax.all_gather(left_blocks, 'row', axis=1, tiled=True)  89 us
    scatter-add x1, other arithmetic, place_terms(): return summed.at[rows, index].add(terms, mode='drop')  52.4 us
    gather x2, local copies, waits for them, and re-layouts, local(): chosen = jnp.take(piece_blocks[:, 0], local_index, axis=0)  33.5 us
    dot_general x1, local copies, waits for them, and re-layouts, local(): jnp.einsum('isxy,isyz->isxz', panel_blocks, chosen, preferred_element_typ...  24.7 us
    dot_general x1, matrix products, local(): jnp.einsum('isxy,isyz->isxz', panel_blocks, chosen, preferred_element_typ...  22.1 us
    squeeze x1, blocking collectives, local(): targets = jnp.take(piece_cols[:, 0], local_index, axis=0) - row_rank * NJR  11.1 us
    all_gather x1, blocking collectives, local(): lax.all_gather(left_cols, 'row', axis=1, tiled=True)  9.8 us
  transfers between devices with their start and end apart: 2, of which 2 were waited for; matrix products, arithmetic and copies ran while one was open for 10% of the time, Pallas kernels for 0%

commit v1 on v0

--- a/solution.py
+++ b/solution.py
@@ -33,7 +33,16 @@
         jnp.float32,
     )
     start = jnp.int32(0)
-    piece_blocks = lax.all_gather(right_blocks, "col", axis=0, tiled=True)
+    n = jax.lax.axis_size("col")
+    pool = [(jj, (jj + 1) % n) for jj in range(n)]
+    mixed_arr, block_next = ([right_blocks], [right_blocks])
+    chunks = [(jj, (jj - 1) % n) for jj in range(n)]
+    for _ in range(n // 2):
+        mixed_arr.append(jax.lax.ppermute(mixed_arr[-1], axis_name="col", perm=pool))
+    for _ in range((n - 1) // 2):
+        block_next.append(jax.lax.ppermute(block_next[-1], perm=chunks, axis_name="col"))
+    res = jnp.concatenate([*mixed_arr[::-1], *block_next[1:]], 0)
+    piece_blocks = jnp.roll(res, (jax.lax.axis_index("col") - n // 2) * right_blocks.shape[0], 0)
     piece_cols = lax.all_gather(right_cols, "col", axis=0, tiled=True)
     local_index = panel_cols - start
     chosen = jnp.take(piece_blocks[:, 0], local_index, axis=0)

time: 395 us -> 368 us (0.932)
  waiting for transfers between devices: 218 us -> 120 us
  local copies, waits for them, and re-layouts: 63.7 us -> 97.6 us
  blocking collectives: 20.9 us -> 47 us
  starting transfers between devices: 0.04 us -> 10.1 us
    all_gather x1 -> x0, waiting for transfers between devices: 128 us -> none  [local(): piece_blocks = lax.all_gather(right_blocks, 'col', axis=0, tiled=True)]
    ppermute x0 -> x7, waiting for transfers between devices: none -> 119 us  [the longest x4 119 us: local(): jax.lax.ppermute(mixed_arr[-1], axis_name='col', perm=pool)]
    all_gather x1, waiting for transfers between devices: 89 us -> 0.01 us  [local(): lax.all_gather(left_blocks, 'row', axis=1, tiled=True)]
    squeeze x1, blocking collectives: 11.1 us -> 38.5 us  [local(): targets = jnp.take(piece_cols[:, 0], local_index, axis=0) - row_rank * NJR]
    unnamed x5 -> x28, local copies, waits for them, and re-layouts: 2.01 us -> 27.4 us
    ppermute x0 -> x7, starting transfers between devices: none -> 10.1 us  [the longest x3 9.57 us: local(): jax.lax.ppermute(block_next[-1], perm=chunks, axis_name='col')]
    squeeze x0 -> x1, local copies, waits for them, and re-layouts: none -> 6.51 us  [local(): chosen = jnp.take(piece_blocks[:, 0], local_index, axis=0)]
  transfers between devices with their start and end apart: 2 -> 8, of which waited for: 2 -> 3; matrix products, arithmetic and copies ran while one was open for 10% -> 19% of each run, Pallas kernels for 0% -> 0%
where the time goes in v1:
time: 368 us; the launch traced here: 366 us
  waiting for transfers between devices  120 us (33%)
  local copies, waits for them, and re-layouts  97.6 us (27%)
  other arithmetic  54.7 us (15%)
  blocking collectives  47 us (13%)
  matrix products  22.1 us (6%)
  between operations  14.3 us (4%)
  starting transfers between devices  10.1 us (3%)
    ppermute x4, waiting for transfers between devices, local(): jax.lax.ppermute(mixed_arr[-1], axis_name='col', perm=pool)  119 us
    scatter-add x1, other arithmetic, place_terms(): return summed.at[rows, index].add(terms, mode='drop')  52.4 us
    squeeze x1, blocking collectives, local(): targets = jnp.take(piece_cols[:, 0], local_index, axis=0) - row_rank * NJR  38.5 us
    gather x2, local copies, waits for them, and re-layouts, local(): chosen = jnp.take(piece_blocks[:, 0], local_index, axis=0)  33.6 us
    unnamed x28, local copies, waits for them, and re-layouts  27.4 us
    dot_general x1, local copies, waits for them, and re-layouts, local(): jnp.einsum('isxy,isyz->isxz', panel_blocks, chosen, preferred_element_typ...  24.6 us
    dot_general x1, matrix products, local(): jnp.einsum('isxy,isyz->isxz', panel_blocks, chosen, preferred_element_typ...  22.1 us
    ppermute x3, starting transfers between devices, local(): jax.lax.ppermute(block_next[-1], perm=chunks, axis_name='col')  9.57 us
  transfers between devices with their start and end apart: 8, of which 3 were waited for; matrix products, arithmetic and copies ran while one was open for 19% of the time, Pallas kernels for 0%

profile of v1, /device:TPU:0, one launch (start us, length us, event | category | flops | bytes accessed | tf_op | source)
XLA Modules:
  0.0 365.9 jit_solution(4340983148164523889)
XLA Ops:
  6.5 0.0 copy-start
  6.5 0.0 all-gather.2.cloned.1.call-start
  6.5 0.7 all-gather.2.cloned.1.call-update
  7.3 0.5 collective-permute-start
  7.8 28.0 %collective-permute-done = bf16[64,1,128,128]{3,2,1,0:T(8,128)(2,1)S(1)} collective-permute-done((bf16[64,1,128,128]{3,2,1,0:T(8,128)(2,1)}, bf16[64,1,128,128]{3,2,1,0:T(8,128)(2,1)S(1)}, u32[]{:S(2)}, u32[]{:S(2)}) %collective-permute-start) | collective-permute-done | bytes 2097184 | tf_op jit(solution)/shard_map/ppermute | solution.py:41
  35.8 0.0 copy-start.1
  35.8 1.3 copy-done.1
  37.1 0.0 collective-permute-start.1
  37.1 3.5 collective-permute-start.4
  40.6 45.3 %collective-permute-done.1 = bf16[64,1,128,128]{3,2,1,0:T(8,128)(2,1)S(1)} collective-permute-done((bf16[64,1,128,128]{3,2,1,0:T(8,128)(2,1)S(1)}, bf16[64,1,128,128]{3,2,1,0:T(8,128)(2,1)S(1)}, u32[]{:S(2)}, u32[]{:S(2)}) %collective-permute-start.1) | collective-permute-done | bytes 2097184 | tf_op jit(solution)/shard_map/ppermute | solution.py:41
  85.9 0.0 copy-start.3
  85.9 1.3 copy-done.3
  87.2 0.0 collective-permute-start.2
  87.2 0.0 collective-permute-done.4
  87.2 3.5 collective-permute-start.5
  90.8 46.1 %collective-permute-done.2 = bf16[64,1,128,128]{3,2,1,0:T(8,128)(2,1)} collective-permute-done((bf16[64,1,128,128]{3,2,1,0:T(8,128)(2,1)S(1)}, bf16[64,1,128,128]{3,2,1,0:T(8,128)(2,1)}, u32[]{:S(2)}, u32[]{:S(2)}) %collective-permute-start.2) | collective-permute-done | bytes 2097184 | tf_op jit(solution)/shard_map/ppermute | solution.py:41
  136.9 0.0 collective-permute-start.3
  136.9 8.5 %all_gather.9 = s32[12,32]{0,1:T(8,128)S(1)} all-gather(s32[12,8]{0,1:T(8,128)} %param.6), channel_id=1, replica_groups=mesh['row'=4,'col'=8] {'row'}, dimensions={1}, use_global_device_ids=true | all-gather | bytes 1920 | tf_op jit(solution)/shard_map/all_gather | solution.py:29
  145.4 0.1 copy.20
  145.5 0.1 reshape.46
  145.6 1.2 dynamic-slice
  147.5 0.8 bitcast_dynamic-update-slice_fusion
  148.2 0.0 collective-permute-done.5
  148.2 2.5 collective-permute-start.6
  150.7 38.5 %all-reduce = s32[512]{0:T(512)S(1)} all-reduce(s32[512]{0:T(512)S(1)} %bitcast_dynamic-update-slice_fusion), channel_id=1, replica_groups=mesh['row'=4,'col'=8] {'col'}, use_global_device_ids=true, to_apply=%add | all-reduce | flops 512 | bytes 4096 | tf_op jit(solution)/shard_map/squeeze | solution.py:49
  189.2 2.8 gather_fusion
  192.0 0.1 reshape.45
  192.1 0.7 broadcast_subtract_fusion
  192.8 0.1 copy.23
  192.9 0.1 fusion.4
  193.0 0.1 compare_reduce_fusion
  193.1 0.1 reshape.60
  193.2 0.0 copy-start.4
  193.2 0.0 copy-start.2
  193.2 0.0 collective-permute-done.3
  193.2 1.9 constant_dynamic-update-slice_fusion.15
  195.1 2.0 constant_dynamic-update-slice_fusion.14
  197.1 2.0 constant_dynamic-update-slice_fusion.13
  199.1 2.0 constant_dynamic-update-slice_fusion.12
  201.0 0.0 copy-done
  201.0 0.3 constant_dynamic-update-slice_fusion.11
  201.3 2.0 constant_dynamic-update-slice_fusion.10
  203.3 2.0 constant_dynamic-update-slice_fusion.9
  205.3 0.0 collective-permute-done.6
  205.3 2.0 constant_dynamic-update-slice_fusion.8
  207.3 2.0 constant_dynamic-update-slice_fusion.7
  209.3 2.0 constant_dynamic-update-slice_fusion.6
  211.2 0.0 copy-done.4
  211.2 0.3 constant_dynamic-update-slice_fusion.5
  211.5 0.0 copy-done.2
  211.5 0.3 constant_dynamic-update-slice_fusion.4
  211.8 0.3 constant_dynamic-update-slice_fusion.3
  212.1 2.0 constant_dynamic-update-slice_fusion.2
  214.1 2.0 constant_dynamic-update-slice_fusion.1
  216.1 2.0 constant_dynamic-update-slice_fusion
  218.0 6.5 %dynamic-slice_bitcast_fusion = bf16[512,128,128]{2,1,0:T(8,128)(2,1)} fusion(bf16[1024,1,128,128]{3,2,1,0:T(8,128)(2,1)S(1)} %constant_dynamic-update-slice_fusion, s32[]{:T(128)S(6)} %select_n.62), kind=kLoop, calls=%fused_computation.3 | loop fusion | bytes 33554436 | tf_op jit(solution)/shard_map/squeeze | solution.py:48
  224.5 16.8 %gather_fusion.1 = bf16[384,128,128]{2,1,0:T(8,128)(2,1)} fusion(bf16[512,128,128]{2,1,0:T(8,128)(2,1)} %dynamic-slice_bitcast_fusion, s32[1024]{0:T(1024)S(1)} %pad_clamp_fusion), kind=kCustom, calls=%fused_computation.1 | custom fusion | bytes 25167360 | tf_op jit(solution)/shard_map/jit(_take)/gather | solution.py:48
  241.4 16.7 %copy.24 = bf16[12,32,128,128]{2,3,1,0:T(8,128)(2,1)} copy(bf16[12,32,128,128]{3,2,1,0:T(8,128)(2,1)} %bitcast.17) | data formatting | bytes 25165824 | tf_op jit(solution)/shard_map/jit(_take)/gather | solution.py:48
  258.1 0.0 all-gather.2.cloned.1.call-done
  258.1 22.1 %fusion = f32[12,32,128,128]{3,2,1,0:T(8,128)} fusion(bf16[12,32,128,128]{3,2,1,0:T(8,128)(2,1)} %all-gather.2.cloned.1.call-done, bf16[12,32,128,128]{2,3,1,0:T(8,128)(2,1)} %copy.24, pred[12,32]{1,0:T(8,128)(4,1)S(1)} %get-tuple-element.6), kind=kOutput, calls=%fused_computation.4 | convolution fusion | flops 1616904192 | bytes 50332032 | tf_op jit(solution)/shard_map/isxy,isyz->isxz/dot_general | solution.py:50
  280.2 24.6 %copy.25 = f32[384,128,128]{2,1,0:T(8,128)} copy(f32[384,128,128]{1,2,0:T(8,128)} %bitcast.16) | data formatting | bytes 50331648 | tf_op jit(solution)/shard_map/isxy,isyz->isxz/dot_general | solution.py:50
  304.9 0.4 broadcast_in_dim.38
  305.2 52.4 %scatter_fusion = f32[12,4,128,128]{3,2,1,0:T(8,128)S(1)} fusion(f32[12,4,128,128]{3,2,1,0:T(8,128)S(1)} %broadcast_in_dim.38, s32[384]{0:T(512)S(1)} %reshape.60, f32[384,128,128]{2,1,0:T(8,128)} %copy.25), kind=kCustom, calls=%fused_computation.2 | custom fusion | flops 6291456 | bytes 75500544 | tf_op jit(solution)/shard_map/scatter-add | solution.py:21
  357.7 1.4 convert_element_type.4
  (5 shorter events, 0.0 us)
Async XLA Ops:
  6.5 194.5 %copy-start = (bf16[64,1,128,128]{3,2,1,0:T(8,128)(2,1)S(1)}, bf16[64,1,128,128]{3,2,1,0:T(8,128)(2,1)}, u32[]{:S(2)}) copy-start(bf16[64,1,128,128]{3,2,1,0:T(8,128)(2,1)} %param.7) | copy-start | bytes 6291460
  6.5 251.6 %all-gather.2.cloned.1.call-start = ((), (), s32[]{:S(2)}) async-start(), calls=%async_computation | async-start | bytes 15728640 | tf_op jit(solution)/shard_map/all_gather | solution.py:28
  7.3 28.5 %collective-permute-start = (bf16[64,1,128,128]{3,2,1,0:T(8,128)(2,1)}, bf16[64,1,128,128]{3,2,1,0:T(8,128)(2,1)S(1)}, u32[]{:S(2)}, u32[]{:S(2)}) collective-permute-start(bf16[64,1,128,128]{3,2,1,0:T(8,128)(2,1)} %param.7), channel_id=1, source_target_pairs={{0,1},{1,2},{2,3},{3,4},{4,5},{5,6},{6,7},{7,0},{8,9},{9,10},{10,1... | collective-permute-start | bytes 6291464 | tf_op jit(solution)/shard_map/ppermute | solution.py:41
  35.8 1.3 copy-start.1
  37.1 48.8 %collective-permute-start.1 = (bf16[64,1,128,128]{3,2,1,0:T(8,128)(2,1)S(1)}, bf16[64,1,128,128]{3,2,1,0:T(8,128)(2,1)S(1)}, u32[]{:S(2)}, u32[]{:S(2)}) collective-permute-start(bf16[64,1,128,128]{3,2,1,0:T(8,128)(2,1)S(1)} %collective-permute-done), channel_id=1, source_target_pairs={{0,1},{1,2},{2,3},{3,4},{4,5},{5,6},{6,7},{7,0},{8,9},{9,10},{10,1... | collective-permute-start | bytes 6291464 | tf_op jit(solution)/shard_map/ppermute | solution.py:41
  37.1 50.1 %collective-permute-start.4 = (bf16[64,1,128,128]{3,2,1,0:T(8,128)(2,1)}, bf16[64,1,128,128]{3,2,1,0:T(8,128)(2,1)}, u32[]{:S(2)}, u32[]{:S(2)}) collective-permute-start(bf16[64,1,128,128]{3,2,1,0:T(8,128)(2,1)} %param.7), channel_id=1, source_target_pairs={{0,7},{1,0},{2,1},{3,2},{4,3},{5,4},{6,5},{7,6},{8,15},{9,8},{10,9... | collective-permute-start | bytes 6291464 | tf_op jit(solution)/shard_map/ppermute | solution.py:43
  85.9 1.3 copy-start.3
  87.2 49.7 %collective-permute-start.2 = (bf16[64,1,128,128]{3,2,1,0:T(8,128)(2,1)S(1)}, bf16[64,1,128,128]{3,2,1,0:T(8,128)(2,1)}, u32[]{:S(2)}, u32[]{:S(2)}) collective-permute-start(bf16[64,1,128,128]{3,2,1,0:T(8,128)(2,1)S(1)} %collective-permute-done.1), channel_id=1, source_target_pairs={{0,1},{1,2},{2,3},{3,4},{4,5},{5,6},{6,7},{7,0},{8,9},{9,10},{10,1... | collective-permute-start | bytes 6291464 | tf_op jit(solution)/shard_map/ppermute | solution.py:41
  87.2 61.0 %collective-permute-start.5 = (bf16[64,1,128,128]{3,2,1,0:T(8,128)(2,1)}, bf16[64,1,128,128]{3,2,1,0:T(8,128)(2,1)}, u32[]{:S(2)}, u32[]{:S(2)}) collective-permute-start(bf16[64,1,128,128]{3,2,1,0:T(8,128)(2,1)} %collective-permute-done.4), channel_id=1, source_target_pairs={{0,7},{1,0},{2,1},{3,2},{4,3},{5,4},{6,5},{7,6},{8,15},{9,8},{10,9... | collective-permute-start | bytes 6291464 | tf_op jit(solution)/shard_map/ppermute | solution.py:43
  136.9 56.3 %collective-permute-start.3 = (bf16[64,1,128,128]{3,2,1,0:T(8,128)(2,1)}, bf16[64,1,128,128]{3,2,1,0:T(8,128)(2,1)}, u32[]{:S(2)}, u32[]{:S(2)}) collective-permute-start(bf16[64,1,128,128]{3,2,1,0:T(8,128)(2,1)} %collective-permute-done.2), channel_id=1, source_target_pairs={{0,1},{1,2},{2,3},{3,4},{4,5},{5,6},{6,7},{7,0},{8,9},{9,10},{10,1... | collective-permute-start | bytes 6291464 | tf_op jit(solution)/shard_map/ppermute | solution.py:41
  148.2 57.0 %collective-permute-start.6 = (bf16[64,1,128,128]{3,2,1,0:T(8,128)(2,1)}, bf16[64,1,128,128]{3,2,1,0:T(8,128)(2,1)}, u32[]{:S(2)}, u32[]{:S(2)}) collective-permute-start(bf16[64,1,128,128]{3,2,1,0:T(8,128)(2,1)} %collective-permute-done.5), channel_id=1, source_target_pairs={{0,7},{1,0},{2,1},{3,2},{4,3},{5,4},{6,5},{7,6},{8,15},{9,8},{10,9... | collective-permute-start | bytes 6291464 | tf_op jit(solution)/shard_map/ppermute | solution.py:43
  193.2 18.0 %copy-start.4 = (bf16[64,1,128,128]{3,2,1,0:T(8,128)(2,1)S(1)}, bf16[64,1,128,128]{3,2,1,0:T(8,128)(2,1)}, u32[]{:S(2)}) copy-start(bf16[64,1,128,128]{3,2,1,0:T(8,128)(2,1)} %copy-done.3) | copy-start | bytes 6291460
  193.2 18.3 %copy-start.2 = (bf16[64,1,128,128]{3,2,1,0:T(8,128)(2,1)S(1)}, bf16[64,1,128,128]{3,2,1,0:T(8,128)(2,1)}, u32[]{:S(2)}) copy-start(bf16[64,1,128,128]{3,2,1,0:T(8,128)(2,1)} %copy-done.1) | copy-start | bytes 6291460
Sparse Core Ops, SparseCore 0:
  9.2 125.1 all-gather.1
